TPU v7x, 32 devices: a whole 2x2x4 slice. The times are simulated.
32 devices in a mesh: narrow: 8 (over z, x), wide: 4 (over y, core).
Axes of the slice: x: 2, y: 2, z: 4, core: 2. Of those that a mesh axis runs over, the one named last changes fastest.
Arguments:
- amps: bfloat16 [16, 512, 512], P(None, 'narrow', 'wide'), may hold values from -1 to 1
- left_fit: bfloat16 [64, 512, 256], P(None, 'narrow'), may hold values from -0.375 to 0.375
- right_fit: bfloat16 [512, 512, 256], P('narrow', 'wide'), may hold values from -0.375 to 0.375
- pair_list: int32 [16, 2], P('narrow'), may hold values from 0 to 127, as said below
- occ_energy: float32 [128], replicated, may hold values from -2 to -0.5
- vir_energy: float32 [512], replicated, may hold values from 0.5 to 3
Outputs:
- update: float32 [16, 64, 512], P('narrow', None, 'wide')
Inputs may be any that keep to these rules, and one draw needn't show every extreme that they name: `pair_list`: each row (i, j) has i <= j.
All inputs are finite; a program needn't handle non-finite values.
Results may differ from a plain program's by a relative error of at most 0.0029.
Values may be sent and summed in bfloat16 or wider, within the bound.
No kernel may reach another device: no remote copies, remote signals or barrier semaphores. Data moves between devices by JAX's collectives and lax.ppermute only.
A program may use at most 128 MiB of HBM per device.

v0:
```python
import jax
import jax.numpy as jnp
from jax import lax
from jax.sharding import PartitionSpec as P


def body(amps, left_fit, right_fit, pair_list, occ_energy, vir_energy):
    right_all = lax.all_gather(right_fit, "narrow", axis=0, tiled=True)
    vir_total, col_width, aux_width = right_all.shape
    right_mat = right_all.reshape(vir_total, col_width * aux_width)
    rows_total = left_fit.shape[0]
    amps_full = lax.all_to_all(amps, "narrow", split_axis=0, concat_axis=1, tiled=True)
    pairs_here = amps_full.shape[0]
    partials = []
    for start_row in range(0, rows_total, 16):
        row_block = left_fit[start_row : start_row + 16]
        running = jnp.einsum(
            "acq,pcd->padq",
            lax.all_gather(row_block, "narrow", axis=1, tiled=True),
            amps_full,
            preferred_element_type=jnp.float32,
        )
        rows_here = running.shape[1]
        mixed_rows = running.astype(jnp.bfloat16).reshape(
            pairs_here * rows_here, col_width * aux_width
        )
        project_ladder_part = lax.dot_general(
            mixed_rows, right_mat, (((1,), (1,)), ((), ())), preferred_element_type=jnp.float32
        )
        partials.append(project_ladder_part.reshape(pairs_here, rows_here, vir_total))
    reduced = [
        lax.psum_scatter(ladder_part, "wide", scatter_dimension=2, tiled=True)
        for ladder_part in partials
    ]
    ladder_sum = jnp.concatenate(reduced, axis=1)
    local_cols = ladder_sum.shape[2]
    occ_ids = jnp.arange(occ_energy.shape[0], dtype=jnp.int32)
    occ_first = jnp.sum(
        jnp.where(pair_list[:, 0:1] == occ_ids[None, :], occ_energy[None, :], 0.0), axis=1
    )
    occ_second = jnp.sum(
        jnp.where(pair_list[:, 1:2] == occ_ids[None, :], occ_energy[None, :], 0.0), axis=1
    )
    vir_cols = lax.dynamic_slice_in_dim(
        vir_energy, lax.axis_index("wide") * local_cols, local_cols, 0
    )
    vir_rows = vir_energy[:rows_total]
    denominator = (
        (occ_first + occ_second)[:, None, None] - vir_rows[None, :, None] - vir_cols[None, None, :]
    )
    return ladder_sum / denominator


def solution(mesh):
    return jax.shard_map(
        body,
        mesh=mesh,
        in_specs=(
            P(None, "narrow", "wide"),
            P(None, "narrow", None),
            P("narrow", "wide", None),
            P("narrow", None),
            P(),
            P(),
        ),
        out_specs=P("narrow", None, "wide"),
        check_vma=False,
    )
```

profile of v0, /device:TPU:0, one launch (start us, length us, event | category | flops | bytes accessed | tf_op | source)
XLA Modules:
  0.0 1060.1 jit_solution(1422802223781420822)
XLA Ops:
  6.5 2.9 fusion.50
  9.5 0.0 all-gather.12.cloned.1.call-start
  9.5 0.7 all-gather.12.cloned.1.call-update
  10.2 0.0 all-gather.10.cloned.1.call-start
  10.3 0.7 all-gather.10.cloned.1.call-update
  11.0 0.5 all-gather.6.cloned.1.call-update
  11.6 6.5 copy.21
  18.1 7.4 all-to-all-start
  25.6 0.1 dynamic_slice.3
  25.7 0.2 slice_reduce_fusion
  25.8 0.2 fusion.49
  26.1 16.1 %all-to-all-done = bf16[16,64,128]{2,1,0:T(8,128)(2,1)S(1)} async-done(((bf16[16,64,128]{2,1,0:T(8,128)(2,1)}), bf16[16,64,128]{2,1,0:T(8,128)(2,1)S(1)}, u32[]{:S(2)}, u32[]{:S(2)}) %all-to-all-start) | async-done | bytes 262176 | tf_op jit(solution)/shard_map/all_to_all | solution.py:12
  42.2 49.1 %all-gather.14.cloned.1.call-done = bf16[16,512,256]{2,1,0:T(8,128)(2,1)} async-done(((bf16[16,64,256]{2,1,0:T(8,128)(2,1)}), bf16[16,512,256]{2,1,0:T(8,128)(2,1)}) %all-gather.14.cloned.1.call-update) | async-done | bytes 4194320 | tf_op jit(solution)/shard_map/all_gather | solution.py:19
  91.2 4.8 convert_bitcast_fusion
  96.0 69.1 %all-gather.12.cloned.1.call-done = bf16[16,512,256]{2,1,0:T(8,128)(2,1)} async-done(((bf16[16,64,256]{2,1,0:T(8,128)(2,1)}), bf16[16,512,256]{2,1,0:T(8,128)(2,1)}) %all-gather.12.cloned.1.call-update) | async-done | bytes 4194320 | tf_op jit(solution)/shard_map/all_gather | solution.py:19
  165.1 4.8 convert_bitcast_fusion.1
  169.9 69.1 %all-gather.10.cloned.1.call-done = bf16[16,512,256]{2,1,0:T(8,128)(2,1)} async-done(((bf16[16,64,256]{2,1,0:T(8,128)(2,1)}), bf16[16,512,256]{2,1,0:T(8,128)(2,1)}) %all-gather.10.cloned.1.call-update) | async-done | bytes 4194320 | tf_op jit(solution)/shard_map/all_gather | solution.py:19
  239.0 4.9 convert_bitcast_fusion.2
  243.8 68.9 %all-gather.6.cloned.1.call-done = bf16[16,512,256]{2,1,0:T(8,128)(2,1)} async-done(((bf16[16,64,256]{2,1,0:T(8,128)(2,1)}), bf16[16,512,256]{2,1,0:T(8,128)(2,1)}) %all-gather.6.cloned.1.call-update) | async-done | bytes 4194320 | tf_op jit(solution)/shard_map/all_gather | solution.py:19
  312.7 3.5 convert_bitcast_fusion.3
  316.2 634.0 %all-gather.8.cloned.1.call-done = bf16[512,128,256]{2,0,1:T(8,128)(2,1)} async-done(((bf16[64,128,256]{2,0,1:T(8,128)(2,1)}), bf16[512,128,256]{2,0,1:T(8,128)(2,1)}) %all-gather.8.cloned.1.call-update) | async-done | bytes 33554448 | tf_op jit(solution)/shard_map/all_gather | solution.py:8
  950.1 16.3 %fusion.43 = f32[2,16,512]{2,1,0:T(8,128)} fusion(bf16[512,128,256]{2,0,1:T(8,128)(2,1)} %all-gather.8.cloned.1.call-done, bf16[2,16,128,256]{3,2,1,0:T(8,128)(2,1)} %convert_bitcast_fusion), kind=kOutput, calls=%fused_computation.27 | convolution fusion | flops 1073741824 | bytes 35717120 | tf_op jit(solution)/shard_map/dot_general | solution.py:27
  966.4 0.0 reduce-scatter.9.cloned.1.call-start
  966.5 16.3 %fusion.38 = f32[2,16,512]{2,1,0:T(8,128)} fusion(bf16[512,128,256]{2,0,1:T(8,128)(2,1)} %all-gather.8.cloned.1.call-done, bf16[2,16,128,256]{3,2,1,0:T(8,128)(2,1)} %convert_bitcast_fusion.1), kind=kOutput, calls=%fused_computation.26 | convolution fusion | flops 1073741824 | bytes 35717120 | tf_op jit(solution)/shard_map/dot_general | solution.py:27
  982.8 0.2 reduce-scatter.7.cloned.1.call-start
  983.0 16.3 %fusion.33 = f32[2,16,512]{2,1,0:T(8,128)} fusion(bf16[512,128,256]{2,0,1:T(8,128)(2,1)} %all-gather.8.cloned.1.call-done, bf16[2,16,128,256]{3,2,1,0:T(8,128)(2,1)} %convert_bitcast_fusion.2), kind=kOutput, calls=%fused_computation.25 | convolution fusion | flops 1073741824 | bytes 35717120 | tf_op jit(solution)/shard_map/dot_general | solution.py:27
  999.4 0.0 reduce-scatter.5.cloned.1.call-start
  999.4 15.9 %fusion.28 = f32[2,16,512]{2,1,0:T(8,128)} fusion(bf16[512,128,256]{2,0,1:T(8,128)(2,1)} %all-gather.8.cloned.1.call-done, bf16[2,16,128,256]{3,2,1,0:T(8,128)(2,1)S(1)} %convert_bitcast_fusion.3), kind=kOutput, calls=%fused_computation.24 | convolution fusion | flops 1073741824 | bytes 35717120 | tf_op jit(solution)/shard_map/dot_general | solution.py:27
  1015.4 0.1 broadcast_subtract_fusion
  1015.5 14.6 %reduce-scatter.7.cloned.1.call-done = f32[2,16,128]{2,1,0:T(8,128)} async-done(((f32[2,16,512]{2,1,0:T(8,128)}), f32[2,16,128]{2,1,0:T(8,128)}) %reduce-scatter.7.cloned.1.call-update) | async-done | bytes 16400 | tf_op jit(solution)/shard_map/reduce_scatter | solution.py:32
  1030.0 22.0 %reduce-scatter.5.cloned.1.call-done = f32[2,16,128]{2,1,0:T(8,128)} async-done(((f32[2,16,512]{2,1,0:T(8,128)}), f32[2,16,128]{2,1,0:T(8,128)}) %reduce-scatter.5.cloned.1.call-update) | async-done | bytes 16400 | tf_op jit(solution)/shard_map/reduce_scatter | solution.py:32
  1052.1 1.5 maximum_divide_fusion
  (22 shorter events, 0.3 us)
Async XLA Ops:
  6.5 84.7 %all-gather.14.cloned.1.call-start = ((), (), s32[]{:S(2)}) async-start(), calls=%async_computation.12 | async-start | bytes 4718592 | tf_op jit(solution)/shard_map/all_gather | solution.py:19
  9.5 155.6 %all-gather.12.cloned.1.call-start = ((), (), s32[]{:S(2)}) async-start(), calls=%async_computation.10 | async-start | bytes 4718592 | tf_op jit(solution)/shard_map/all_gather | solution.py:19
  10.2 228.8 %all-gather.10.cloned.1.call-start = ((), (), s32[]{:S(2)}) async-start(), calls=%async_computation.8 | async-start | bytes 4718592 | tf_op jit(solution)/shard_map/all_gather | solution.py:19
  11.0 301.7 %all-gather.6.cloned.1.call-start = ((), (), s32[]{:S(2)}) async-start(), calls=%async_computation.5 | async-start | bytes 4718592 | tf_op jit(solution)/shard_map/all_gather | solution.py:19
  11.5 938.6 %all-gather.8.cloned.1.call-start = ((), (), s32[]{:S(2)}) async-start(), calls=%async_computation.6 | async-start | bytes 37748736 | tf_op jit(solution)/shard_map/all_gather | solution.py:8
  18.1 7.5 copy-start.2
  18.1 7.6 copy-start
  18.1 7.7 copy-start.1
  18.1 24.0 %all-to-all-start = ((bf16[16,64,128]{2,1,0:T(8,128)(2,1)}), bf16[16,64,128]{2,1,0:T(8,128)(2,1)S(1)}, u32[]{:S(2)}, u32[]{:S(2)}) async-start(bf16[16,64,128]{2,1,0:T(8,128)(2,1)} %param.6), calls=%async_computation | async-start | bytes 524288 | tf_op jit(solution)/shard_map/all_to_all | solution.py:12
  25.5 989.9 %reduce-scatter.11.cloned.1.call-start = ((), (), s32[]{:S(2)}) async-start(), calls=%async_computation.13 | async-start | bytes 81920 | tf_op jit(solution)/shard_map/reduce_scatter | solution.py:32
  966.4 49.0 %reduce-scatter.9.cloned.1.call-start = ((), (), s32[]{:S(2)}) async-start(), calls=%async_computation.11 | async-start | bytes 81920 | tf_op jit(solution)/shard_map/reduce_scatter | solution.py:32
  982.8 47.2 %reduce-scatter.7.cloned.1.call-start = ((), (), s32[]{:S(2)}) async-start(), calls=%async_computation.9 | async-start | bytes 81920 | tf_op jit(solution)/shard_map/reduce_scatter | solution.py:32
  999.4 16.0 %slice-start = ((f32[512]{0:T(512)}), f32[64]{0:T(128)S(1)}, s32[]{:S(2)}) async-start(f32[512]{0:T(512)} %param.11), calls=%async_computation.14 | async-start | bytes 1024 | tf_op jit(solution)/shard_map/slice | solution.py:47
  999.4 52.7 %reduce-scatter.5.cloned.1.call-start = ((), (), s32[]{:S(2)}) async-start(), calls=%async_computation.7 | async-start | bytes 81920 | tf_op jit(solution)/shard_map/reduce_scatter | solution.py:32
Sparse Core Ops, SparseCore 0:
  9.6 81.6 all-gather.13
  93.4 71.6 all-gather.11
  167.3 71.6 all-gather.9
  241.0 71.6 all-gather.5
  314.1 635.9 all-gather.7
  966.5 19.4 reduce-scatter.10
  988.6 19.4 reduce-scatter.8
  1010.5 19.5 reduce-scatter.6
  1032.6 19.4 reduce-scatter.4
where the time goes:
time: 1060 us
  waiting for transfers between devices  945 us (89%)
  matrix products  82.7 us (8%)
  between operations  13.3 us (1%)
    all_gather x1, waiting for transfers between devices, body(): right_all = lax.all_gather(right_fit, 'narrow', axis=0, tiled=True)  634 us
    all_gather x4, waiting for transfers between devices, body(): lax.all_gather(row_block, 'narrow', axis=1, tiled=True)  256 us
    dot_general x4, matrix products, body(): lax.dot_general(mixed_rows, right_mat, (((1,), (1,)), ((), ())), preferre...  64.8 us
    reduce_scatter x4, waiting for transfers between devices, body(): lax.psum_scatter(ladder_part, 'wide', scatter_dimension=2, tiled=True)  36.6 us
  transfers between devices with their start and end apart: 10, of which 8 were waited for; matrix products, arithmetic and copies ran while one was open for 7% of the time, Pallas kernels for 0%

commit v1 on v0

--- a/solution.py
+++ b/solution.py
@@ -5,7 +5,14 @@
 
 
 def body(amps, left_fit, right_fit, pair_list, occ_energy, vir_energy):
-    right_all = lax.all_gather(right_fit, "narrow", axis=0, tiled=True)
+    peers = lax.axis_size("narrow")
+    route = [(i, (i + 1) % peers) for i in range(peers)]
+    terms = [right_fit]
+    for far in range(1, peers):
+        terms = [lax.ppermute(terms[0], "narrow", route), *terms]
+    result = jnp.concatenate(terms, axis=0)
+    offset = (lax.axis_index("narrow") + 1) * terms[-1].shape[0]
+    right_all = jnp.roll(result, offset, axis=0)
     vir_total, col_width, aux_width = right_all.shape
     right_mat = right_all.reshape(vir_total, col_width * aux_width)
     rows_total = left_fit.shape[0]

time: 1060 us -> 1070 us (level)
  local copies, waits for them, and re-layouts: 9.72 us -> 82.8 us
  waiting for transfers between devices: 945 us -> 883 us
    ppermute x0 -> x7, waiting for transfers between devices: none -> 761 us  [body(): terms = [lax.ppermute(terms[0], 'narrow', route), *terms]]
    all_gather x1 -> x0, waiting for transfers between devices: 634 us -> none  [body(): right_all = lax.all_gather(right_fit, 'narrow', axis=0, tiled=True)]
    all_gather x4, waiting for transfers between devices: 256 us -> 0.03 us  [body(): lax.all_gather(row_block, 'narrow', axis=1, tiled=True)]
    all_to_all x1, waiting for transfers between devices: 16.1 us -> 87.2 us  [body(): lax.all_to_all(amps, 'narrow', split_axis=0, concat_axis=1, tiled=True)]
    unnamed x7 -> x26, local copies, waits for them, and re-layouts: 6.52 us -> 74.9 us
  transfers between devices with their start and end apart: 10 -> 16, of which waited for: 8 -> 9; matrix products, arithmetic and copies ran while one was open for 7% -> 7% of each run, Pallas kernels for 0% -> 0%
where the time goes in v1:
time: 1070 us
  waiting for transfers between devices  883 us (83%)
  local copies, waits for them, and re-layouts  82.8 us (8%)
  matrix products  82.4 us (8%)
  between operations  13.6 us (1%)
    ppermute x7, waiting for transfers between devices, body(): terms = [lax.ppermute(terms[0], 'narrow', route), *terms]  761 us
    all_to_all x1, waiting for transfers between devices, body(): lax.all_to_all(amps, 'narrow', split_axis=0, concat_axis=1, tiled=True)  87.2 us
    unnamed x26, local copies, waits for them, and re-layouts  74.9 us
    dot_general x4, matrix products, body(): lax.dot_general(mixed_rows, right_mat, (((1,), (1,)), ((), ())), preferre...  64.5 us
    reduce_scatter x4, waiting for transfers between devices, body(): lax.psum_scatter(ladder_part, 'wide', scatter_dimension=2, tiled=True)  34.7 us
  transfers between devices with their start and end apart: 16, of which 9 were waited for; matrix products, arithmetic and copies ran while one was open for 7% of the time, Pallas kernels for 0%

profile of v1, /device:TPU:0, one launch (start us, length us, event | category | flops | bytes accessed | tf_op | source)
XLA Modules:
  0.0 1072.8 jit_solution(2306669467824012857)
XLA Ops:
  17.1 144.4 %collective-permute-done = bf16[64,128,256]{2,0,1:T(8,128)(2,1)} collective-permute-done((bf16[64,128,256]{2,0,1:T(8,128)(2,1)S(1)}, bf16[64,128,256]{2,0,1:T(8,128)(2,1)}, u32[]{:S(2)}, u32[]{:S(2)}) %collective-permute-start) | collective-permute-done | bytes 4194336 | tf_op jit(solution)/shard_map/ppermute | solution.py:12
  161.6 145.3 %collective-permute-done.1 = bf16[64,128,256]{2,0,1:T(8,128)(2,1)} collective-permute-done((bf16[64,128,256]{2,0,1:T(8,128)(2,1)}, bf16[64,128,256]{2,0,1:T(8,128)(2,1)}, u32[]{:S(2)}, u32[]{:S(2)}) %collective-permute-start.1) | collective-permute-done | bytes 4194336 | tf_op jit(solution)/shard_map/ppermute | solution.py:12
  306.9 93.8 %collective-permute-done.2 = bf16[64,128,256]{2,0,1:T(8,128)(2,1)} collective-permute-done((bf16[64,128,256]{2,0,1:T(8,128)(2,1)}, bf16[64,128,256]{2,0,1:T(8,128)(2,1)}, u32[]{:S(2)}, u32[]{:S(2)}) %collective-permute-start.2) | collective-permute-done | bytes 4194336 | tf_op jit(solution)/shard_map/ppermute | solution.py:12
  400.8 143.5 %collective-permute-done.3 = bf16[64,128,256]{2,0,1:T(8,128)(2,1)} collective-permute-done((bf16[64,128,256]{2,0,1:T(8,128)(2,1)}, bf16[64,128,256]{2,0,1:T(8,128)(2,1)}, u32[]{:S(2)}, u32[]{:S(2)}) %collective-permute-start.3) | collective-permute-done | bytes 4194336 | tf_op jit(solution)/shard_map/ppermute | solution.py:12
  544.3 92.0 %collective-permute-done.4 = bf16[64,128,256]{2,0,1:T(8,128)(2,1)} collective-permute-done((bf16[64,128,256]{2,0,1:T(8,128)(2,1)}, bf16[64,128,256]{2,0,1:T(8,128)(2,1)}, u32[]{:S(2)}, u32[]{:S(2)}) %collective-permute-start.4) | collective-permute-done | bytes 4194336 | tf_op jit(solution)/shard_map/ppermute | solution.py:12
  636.3 141.7 %collective-permute-done.5 = bf16[64,128,256]{2,0,1:T(8,128)(2,1)} collective-permute-done((bf16[64,128,256]{2,0,1:T(8,128)(2,1)}, bf16[64,128,256]{2,0,1:T(8,128)(2,1)}, u32[]{:S(2)}, u32[]{:S(2)}) %collective-permute-start.5) | collective-permute-done | bytes 4194336 | tf_op jit(solution)/shard_map/ppermute | solution.py:12
  778.1 6.0 all-to-all-start
  784.8 87.2 %all-to-all-done = bf16[16,64,128]{2,1,0:T(8,128)(2,1)S(1)} async-done(((bf16[16,64,128]{2,1,0:T(8,128)(2,1)}), bf16[16,64,128]{2,1,0:T(8,128)(2,1)S(1)}, u32[]{:S(2)}, u32[]{:S(2)}) %all-to-all-start) | async-done | bytes 262176 | tf_op jit(solution)/shard_map/all_to_all | solution.py:19
  872.0 4.9 convert_bitcast_fusion
  876.9 4.8 convert_bitcast_fusion.1
  881.7 4.8 convert_bitcast_fusion.2
  889.9 4.7 constant_dynamic-update-slice_fusion.15
  894.6 4.7 constant_dynamic-update-slice_fusion.14
  899.3 4.7 constant_dynamic-update-slice_fusion.13
  904.0 4.8 constant_dynamic-update-slice_fusion.12
  908.7 4.7 constant_dynamic-update-slice_fusion.11
  913.4 4.6 constant_dynamic-update-slice_fusion.10
  918.1 4.8 constant_dynamic-update-slice_fusion.9
  927.3 4.7 constant_dynamic-update-slice_fusion.7
  932.0 4.7 constant_dynamic-update-slice_fusion.6
  936.7 4.7 constant_dynamic-update-slice_fusion.5
  941.4 4.7 constant_dynamic-update-slice_fusion.4
  946.1 4.8 constant_dynamic-update-slice_fusion.3
  950.9 4.7 constant_dynamic-update-slice_fusion.2
  955.6 4.7 constant_dynamic-update-slice_fusion.1
  960.3 4.6 constant_dynamic-update-slice_fusion
  964.9 15.9 %fusion.47 = f32[2,16,512]{2,1,0:T(8,128)} fusion(bf16[1024,128,256]{2,0,1:T(8,128)(2,1)} %constant_dynamic-update-slice_fusion, s32[]{:T(128)S(6)} %select_n.24, bf16[2,16,128,256]{3,2,1,0:T(8,128)(2,1)S(1)} %copy-done.1), kind=kOutput, calls=%fused_computation.31 | convolution fusion | flops 1073741824 | bytes 35717124 | tf_op jit(solution)/shard_map/dot_general | solution.py:34
  980.9 16.3 %fusion.42 = f32[2,16,512]{2,1,0:T(8,128)} fusion(bf16[1024,128,256]{2,0,1:T(8,128)(2,1)} %constant_dynamic-update-slice_fusion, s32[]{:T(128)S(6)} %select_n.24, bf16[2,16,128,256]{3,2,1,0:T(8,128)(2,1)} %convert_bitcast_fusion.1), kind=kOutput, calls=%fused_computation.30 | convolution fusion | flops 1073741824 | bytes 35717124 | tf_op jit(solution)/shard_map/dot_general | solution.py:34
  997.3 16.4 %fusion.37 = f32[2,16,512]{2,1,0:T(8,128)} fusion(bf16[1024,128,256]{2,0,1:T(8,128)(2,1)} %constant_dynamic-update-slice_fusion, s32[]{:T(128)S(6)} %select_n.24, bf16[2,16,128,256]{3,2,1,0:T(8,128)(2,1)} %convert_bitcast_fusion.2), kind=kOutput, calls=%fused_computation.29 | convolution fusion | flops 1073741824 | bytes 35717124 | tf_op jit(solution)/shard_map/dot_general | solution.py:34
  1013.7 15.9 %fusion.32 = f32[2,16,512]{2,1,0:T(8,128)} fusion(bf16[1024,128,256]{2,0,1:T(8,128)(2,1)} %constant_dynamic-update-slice_fusion, s32[]{:T(128)S(6)} %select_n.24, bf16[2,16,128,256]{3,2,1,0:T(8,128)(2,1)S(1)} %convert_bitcast_fusion.3), kind=kOutput, calls=%fused_computation.28 | convolution fusion | flops 1073741824 | bytes 35717124 | tf_op jit(solution)/shard_map/dot_general | solution.py:34
  1029.8 12.7 %reduce-scatter.7.cloned.1.call-done = f32[2,16,128]{2,1,0:T(8,128)} async-done(((f32[2,16,512]{2,1,0:T(8,128)}), f32[2,16,128]{2,1,0:T(8,128)}) %reduce-scatter.7.cloned.1.call-update) | async-done | bytes 16400 | tf_op jit(solution)/shard_map/reduce_scatter | solution.py:39
  1042.4 22.0 %reduce-scatter.5.cloned.1.call-done = f32[2,16,128]{2,1,0:T(8,128)} async-done(((f32[2,16,512]{2,1,0:T(8,128)}), f32[2,16,128]{2,1,0:T(8,128)}) %reduce-scatter.5.cloned.1.call-update) | async-done | bytes 16400 | tf_op jit(solution)/shard_map/reduce_scatter | solution.py:39
  (53 shorter events, 21.0 us)
Async XLA Ops:
  6.5 865.5 %all-gather.11.cloned.1.call-start = ((), (), s32[]{:S(2)}) async-start(), calls=%async_computation.11 | async-start | bytes 4718592 | tf_op jit(solution)/shard_map/all_gather | solution.py:26
  9.5 774.8 %copy-start.4 = (f32[512]{0:T(512)S(1)}, f32[512]{0:T(512)}, u32[]{:S(2)}) copy-start(f32[512]{0:T(512)} %param.11) | copy-start | bytes 6148
  9.5 774.9 %copy-start.2 = (s32[2,2]{1,0:T(2,128)S(1)}, s32[2,2]{1,0:T(2,128)}, u32[]{:S(2)}) copy-start(s32[2,2]{1,0:T(2,128)} %param.9) | copy-start | bytes 52
  9.5 775.1 %copy-start.3 = (f32[128]{0:T(128)S(1)}, f32[128]{0:T(128)}, u32[]{:S(2)}) copy-start(f32[128]{0:T(128)} %param.10) | copy-start | bytes 1540
  9.5 867.4 %all-gather.9.cloned.1.call-start = ((), (), s32[]{:S(2)}) async-start(), calls=%async_computation.9 | async-start | bytes 4718592 | tf_op jit(solution)/shard_map/all_gather | solution.py:26
  14.1 147.4 %collective-permute-start = (bf16[64,128,256]{2,0,1:T(8,128)(2,1)S(1)}, bf16[64,128,256]{2,0,1:T(8,128)(2,1)}, u32[]{:S(2)}, u32[]{:S(2)}) collective-permute-start(bf16[64,128,256]{2,0,1:T(8,128)(2,1)S(1)} %copy.27), channel_id=1, source_target_pairs={{0,4},{4,8},{8,12},{12,16},{16,20},{20,24},{24,28},{28,0},{1,5},{5... | collective-permute-start | bytes 12582920 | tf_op jit(solution)/shard_map/ppermute | solution.py:12
  161.5 145.4 %collective-permute-start.1 = (bf16[64,128,256]{2,0,1:T(8,128)(2,1)}, bf16[64,128,256]{2,0,1:T(8,128)(2,1)}, u32[]{:S(2)}, u32[]{:S(2)}) collective-permute-start(bf16[64,128,256]{2,0,1:T(8,128)(2,1)} %collective-permute-done), channel_id=1, source_target_pairs={{0,4},{4,8},{8,12},{12,16},{16,20},{20,24},{24,28},{28,0},{1,5},{5... | collective-permute-start | bytes 12582920 | tf_op jit(solution)/shard_map/ppermute | solution.py:12
  161.5 720.2 %all-gather.7.cloned.1.call-start = ((), (), s32[]{:S(2)}) async-start(), calls=%async_computation.7 | async-start | bytes 4718592 | tf_op jit(solution)/shard_map/all_gather | solution.py:26
  306.9 93.8 %collective-permute-start.2 = (bf16[64,128,256]{2,0,1:T(8,128)(2,1)}, bf16[64,128,256]{2,0,1:T(8,128)(2,1)}, u32[]{:S(2)}, u32[]{:S(2)}) collective-permute-start(bf16[64,128,256]{2,0,1:T(8,128)(2,1)} %collective-permute-done.1), channel_id=1, source_target_pairs={{0,4},{4,8},{8,12},{12,16},{16,20},{20,24},{24,28},{28,0},{1,5},{5... | collective-permute-start | bytes 12582920 | tf_op jit(solution)/shard_map/ppermute | solution.py:12
  400.7 143.6 %collective-permute-start.3 = (bf16[64,128,256]{2,0,1:T(8,128)(2,1)}, bf16[64,128,256]{2,0,1:T(8,128)(2,1)}, u32[]{:S(2)}, u32[]{:S(2)}) collective-permute-start(bf16[64,128,256]{2,0,1:T(8,128)(2,1)} %collective-permute-done.2), channel_id=1, source_target_pairs={{0,4},{4,8},{8,12},{12,16},{16,20},{20,24},{24,28},{28,0},{1,5},{5... | collective-permute-start | bytes 12582920 | tf_op jit(solution)/shard_map/ppermute | solution.py:12
  400.8 485.7 %all-gather.5.cloned.1.call-start = ((), (), s32[]{:S(2)}) async-start(), calls=%async_computation.5 | async-start | bytes 4718592 | tf_op jit(solution)/shard_map/all_gather | solution.py:26
  544.3 92.0 %collective-permute-start.4 = (bf16[64,128,256]{2,0,1:T(8,128)(2,1)}, bf16[64,128,256]{2,0,1:T(8,128)(2,1)}, u32[]{:S(2)}, u32[]{:S(2)}) collective-permute-start(bf16[64,128,256]{2,0,1:T(8,128)(2,1)} %collective-permute-done.3), channel_id=1, source_target_pairs={{0,4},{4,8},{8,12},{12,16},{16,20},{20,24},{24,28},{28,0},{1,5},{5... | collective-permute-start | bytes 12582920 | tf_op jit(solution)/shard_map/ppermute | solution.py:12
  636.3 141.7 %collective-permute-start.5 = (bf16[64,128,256]{2,0,1:T(8,128)(2,1)}, bf16[64,128,256]{2,0,1:T(8,128)(2,1)}, u32[]{:S(2)}, u32[]{:S(2)}) collective-permute-start(bf16[64,128,256]{2,0,1:T(8,128)(2,1)} %collective-permute-done.4), channel_id=1, source_target_pairs={{0,4},{4,8},{8,12},{12,16},{16,20},{20,24},{24,28},{28,0},{1,5},{5... | collective-permute-start | bytes 12582920 | tf_op jit(solution)/shard_map/ppermute | solution.py:12
  778.0 111.9 %collective-permute-start.6 = (bf16[64,128,256]{2,0,1:T(8,128)(2,1)}, bf16[64,128,256]{2,0,1:T(8,128)(2,1)}, u32[]{:S(2)}, u32[]{:S(2)}) collective-permute-start(bf16[64,128,256]{2,0,1:T(8,128)(2,1)} %collective-permute-done.5), channel_id=1, source_target_pairs={{0,4},{4,8},{8,12},{12,16},{16,20},{20,24},{24,28},{28,0},{1,5},{5... | collective-permute-start | bytes 12582920 | tf_op jit(solution)/shard_map/ppermute | solution.py:12
  778.1 93.9 %all-to-all-start = ((bf16[16,64,128]{2,1,0:T(8,128)(2,1)}), bf16[16,64,128]{2,1,0:T(8,128)(2,1)S(1)}, u32[]{:S(2)}, u32[]{:S(2)}) async-start(bf16[16,64,128]{2,1,0:T(8,128)(2,1)} %param.6), calls=%async_computation | async-start | bytes 524288 | tf_op jit(solution)/shard_map/all_to_all | solution.py:19
  784.0 245.7 %reduce-scatter.11.cloned.1.call-start = ((), (), s32[]{:S(2)}) async-start(), calls=%async_computation.12 | async-start | bytes 81920 | tf_op jit(solution)/shard_map/reduce_scatter | solution.py:39
  918.1 4.8 copy-start
  960.3 4.6 copy-start.1
  980.8 49.0 %reduce-scatter.9.cloned.1.call-start = ((), (), s32[]{:S(2)}) async-start(), calls=%async_computation.10 | async-start | bytes 81920 | tf_op jit(solution)/shard_map/reduce_scatter | solution.py:39
  997.2 45.2 %reduce-scatter.7.cloned.1.call-start = ((), (), s32[]{:S(2)}) async-start(), calls=%async_computation.8 | async-start | bytes 81920 | tf_op jit(solution)/shard_map/reduce_scatter | solution.py:39
  1013.7 16.0 %slice-start = ((f32[512]{0:T(512)}), f32[64]{0:T(128)S(1)}, s32[]{:S(2)}) async-start(f32[512]{0:T(512)} %param.11), calls=%async_computation.13 | async-start | bytes 1024 | tf_op jit(solution)/shard_map/slice | solution.py:54
  1013.7 50.8 %reduce-scatter.5.cloned.1.call-start = ((), (), s32[]{:S(2)}) async-start(), calls=%async_computation.6 | async-start | bytes 81920 | tf_op jit(solution)/shard_map/reduce_scatter | solution.py:39
Sparse Core Ops, SparseCore 0:
  9.6 115.5 all-gather.10
  161.6 114.3 all-gather.8
  400.9 113.9 all-gather.6
  636.5 113.5 all-gather.4
  980.9 17.5 reduce-scatter.10
  1001.0 19.4 reduce-scatter.8
  1022.9 19.5 reduce-scatter.6
  1045.0 19.4 reduce-scatter.4
